TPU v7x, 32 devices: a whole 2x2x4 slice. The times are simulated.
32 devices in a mesh: row: 4 (over y, x), col: 8 (over z, core).
Axes of the slice: x: 2, y: 2, z: 4, core: 2. Of those that a mesh axis runs over, the one named last changes fastest.
Arguments:
- left_blocks: bfloat16 [96, 32, 128, 128], P('col', 'row'), may hold values from -0.5 to 0.5
- left_cols: int32 [96, 32], P('col', 'row'), may hold values from 0 to 511, as said below
- right_blocks: bfloat16 [512, 4, 128, 128], P('col', 'row'), may hold values from -6 to 6
- right_cols: int32 [512, 4], P('col', 'row'), may hold values from 0 to 127, as said below
- keep_cols: int32 [96, 16], P('col', 'row'), may hold values from 0 to 127, as said below
Outputs:
- product_blocks: bfloat16 [96, 16, 128, 128], P('col', 'row')
Inputs may be any that keep to these rules, and one draw needn't show every extreme that they name: `left_cols`: slot s of every block row names a block column in [(s // 4) * 64, (s // 4 + 1) * 64); the 4 slots of one range name distinct block columns. `right_cols`: entry [K, n] names a block column in [n * 32, (n + 1) * 32). `keep_cols`: slot k of every block row names a block column in [(k // 4) * 32, (k // 4 + 1) * 32); the 4 slots of one range name distinct block columns.
All inputs are finite; a program needn't handle non-finite values.
Results may differ from a plain program's by a relative error of at most 0.001.
Values may be sent and summed in bfloat16 or wider, within the bound.
No kernel may reach another device: no remote copies, remote signals or barrier semaphores. Data moves between devices by JAX's collectives and lax.ppermute only.
A program may use at most 192 MiB of HBM per device.

v0:
```python
import jax
import jax.numpy as jnp
from jax import lax
from jax.sharding import PartitionSpec as P

NJR = 32


def slot_index(targets, kept):
    match = targets[:, :, None] == kept[:, None, :]
    found = jnp.any(match, axis=2)
    position = jnp.sum(
        match.astype(jnp.int32) * jnp.arange(kept.shape[1], dtype=jnp.int32)[None, None, :], axis=2
    )
    return jnp.where(found, position, kept.shape[1])


def place_terms(summed, terms, targets, kept):
    index = slot_index(targets, kept)
    rows = jnp.broadcast_to(jnp.arange(terms.shape[0], dtype=jnp.int32)[:, None], index.shape)
    return summed.at[rows, index].add(terms, mode="drop")


def local(left_blocks, left_cols, right_blocks, right_cols, keep_cols):
    row_rank = lax.axis_index("row")
    kept = keep_cols - row_rank * NJR
    panel_blocks, panel_cols = (
        lax.all_gather(left_blocks, "row", axis=1, tiled=True),
        lax.all_gather(left_cols, "row", axis=1, tiled=True),
    )
    start_sum = jnp.zeros(
        (panel_blocks.shape[0], keep_cols.shape[1], panel_blocks.shape[2], panel_blocks.shape[3]),
        jnp.float32,
    )
    start = jnp.int32(0)
    piece_blocks = lax.all_gather(right_blocks, "col", axis=0, tiled=True)
    piece_cols = lax.all_gather(right_cols, "col", axis=0, tiled=True)
    local_index = panel_cols - start
    chosen = jnp.take(piece_blocks[:, 0], local_index, axis=0)
    targets = jnp.take(piece_cols[:, 0], local_index, axis=0) - row_rank * NJR
    terms = jnp.einsum("isxy,isyz->isxz", panel_blocks, chosen, preferred_element_type=jnp.float32)
    summed = place_terms(start_sum, terms, targets, kept)
    return summed.astype(jnp.bfloat16)


def solution(mesh):
    in_specs = (
        P("col", "row", None, None),
        P("col", "row"),
        P("col", "row", None, None),
        P("col", "row"),
        P("col", "row"),
    )
    out_specs = P("col", "row", None, None)
    return jax.shard_map(local, mesh=mesh, in_specs=in_specs, out_specs=out_specs, check_vma=False)
```

profile of v0, /device:TPU:0, one launch (start us, length us, event | category | flops | bytes accessed | tf_op | source)
XLA Modules:
  0.0 393.2 jit_solution(15735401039370473601)
XLA Ops:
  6.5 0.0 copy-start
  6.5 0.0 all-gather.3.cloned.1.call-start
  6.5 0.7 all-gather.3.cloned.1.call-update
  7.3 0.0 all-gather.5.cloned.1.call-start
  7.3 0.7 all-gather.5.cloned.1.call-update
  8.0 9.8 %all_gather.12 = s32[12,32]{0,1:T(8,128)S(1)} all-gather(s32[12,8]{0,1:T(8,128)} %param.6), channel_id=1, replica_groups=mesh['row'=4,'col'=8] {'row'}, dimensions={1}, use_global_device_ids=true | all-gather | bytes 1920 | tf_op jit(solution)/shard_map/all_gather | solution.py:29
  17.8 0.1 copy.21
  17.9 0.1 reshape.46
  18.0 1.2 dynamic-slice
  19.9 0.8 bitcast_dynamic-update-slice_fusion
  20.7 11.1 %all-reduce = s32[512]{0:T(512)S(1)} all-reduce(s32[512]{0:T(512)S(1)} %bitcast_dynamic-update-slice_fusion), channel_id=1, replica_groups=mesh['row'=4,'col'=8] {'col'}, use_global_device_ids=true, to_apply=%add | all-reduce | flops 512 | bytes 4096 | tf_op jit(solution)/shard_map/squeeze | solution.py:40
  31.7 2.8 gather_fusion
  34.5 0.1 reshape.45
  34.6 0.0 copy-done
  34.6 0.1 copy.24
  34.7 0.1 fusion.4
  34.8 0.1 compare_reduce_fusion
  34.9 0.1 reshape.60
  35.0 127.9 %all-gather.3.cloned.1.call-done = bf16[512,1,128,128]{3,2,1,0:T(8,128)(2,1)} async-done(((bf16[64,1,128,128]{3,2,1,0:T(8,128)(2,1)}), bf16[512,1,128,128]{3,2,1,0:T(8,128)(2,1)}) %all-gather.3.cloned.1.call-update) | async-done | bytes 16777232 | tf_op jit(solution)/shard_map/all_gather | solution.py:36
  162.9 16.8 %gather_fusion.1 = bf16[384,128,128]{2,1,0:T(8,128)(2,1)} fusion(bf16[512,128,128]{2,1,0:T(8,128)(2,1)} %bitcast.17, s32[1024]{0:T(1024)S(1)} %pad_clamp_fusion), kind=kCustom, calls=%fused_computation.1 | custom fusion | bytes 25167360 | tf_op jit(solution)/shard_map/jit(_take)/gather | solution.py:39
  179.8 16.6 %copy.25 = bf16[12,32,128,128]{2,3,1,0:T(8,128)(2,1)} copy(bf16[12,32,128,128]{3,2,1,0:T(8,128)(2,1)} %bitcast.16) | data formatting | bytes 25165824 | tf_op jit(solution)/shard_map/jit(_take)/gather | solution.py:39
  196.4 89.0 %all-gather.5.cloned.1.call-done = bf16[12,32,128,128]{3,2,1,0:T(8,128)(2,1)} async-done(((bf16[12,8,128,128]{3,2,1,0:T(8,128)(2,1)}), bf16[12,32,128,128]{3,2,1,0:T(8,128)(2,1)}) %all-gather.5.cloned.1.call-update) | async-done | bytes 12582928 | tf_op jit(solution)/shard_map/all_gather | solution.py:28
  285.4 22.1 %fusion = f32[12,32,128,128]{3,2,1,0:T(8,128)} fusion(bf16[12,32,128,128]{3,2,1,0:T(8,128)(2,1)} %all-gather.5.cloned.1.call-done, bf16[12,32,128,128]{2,3,1,0:T(8,128)(2,1)} %copy.25, pred[12,32]{1,0:T(8,128)(4,1)S(1)} %get-tuple-element.6), kind=kOutput, calls=%fused_computation.3 | convolution fusion | flops 1616904192 | bytes 50332032 | tf_op jit(solution)/shard_map/isxy,isyz->isxz/dot_general | solution.py:41
  307.5 24.7 %copy.26 = f32[384,128,128]{2,1,0:T(8,128)} copy(f32[384,128,128]{1,2,0:T(8,128)} %bitcast.15) | data formatting | bytes 50331648 | tf_op jit(solution)/shard_map/isxy,isyz->isxz/dot_general | solution.py:41
  332.2 0.4 broadcast_in_dim.38
  332.5 52.4 %scatter_fusion = f32[12,4,128,128]{3,2,1,0:T(8,128)S(1)} fusion(f32[12,4,128,128]{3,2,1,0:T(8,128)S(1)} %broadcast_in_dim.38, s32[384]{0:T(512)S(1)} %reshape.60, f32[384,128,128]{2,1,0:T(8,128)} %copy.26), kind=kCustom, calls=%fused_computation.2 | custom fusion | flops 6291456 | bytes 75500544 | tf_op jit(solution)/shard_map/scatter-add | solution.py:21
  384.9 1.4 convert_element_type.4
  (6 shorter events, 0.0 us)
Async XLA Ops:
  6.5 28.1 %copy-start = (s32[12,4]{0,1:T(4,128)S(1)}, s32[12,4]{0,1:T(4,128)}, u32[]{:S(2)}) copy-start(s32[12,4]{0,1:T(4,128)} %param.9) | copy-start | bytes 580
  6.5 156.4 %all-gather.3.cloned.1.call-start = ((), (), s32[]{:S(2)}) async-start(), calls=%async_computation | async-start | bytes 18874368 | tf_op jit(solution)/shard_map/all_gather | solution.py:36
  7.3 278.1 %all-gather.5.cloned.1.call-start = ((), (), s32[]{:S(2)}) async-start(), calls=%async_computation.1 | async-start | bytes 15728640 | tf_op jit(solution)/shard_map/all_gather | solution.py:28
Sparse Core Ops, SparseCore 0:
  8.9 153.9 all-gather.2
  164.8 120.5 all-gather.4
where the time goes:
time: 395 us; the launch traced here: 393 us
  waiting for transfers between devices  218 us (55%)
  local copies, waits for them, and re-layouts  63.7 us (16%)
  other arithmetic  54 us (14%)
  matrix products  22.1 us (6%)
  blocking collectives  20.9 us (5%)
  between operations  14.1 us (4%)
    all_gather x1, waiting for transfers between devices, local(): piece_blocks = lax.all_gather(right_blocks, 'col', axis=0, tiled=True)  128 us
    all_gather x1, waiting for transfers between devices, local(): lax.all_gather(left_blocks, 'row', axis=1, tiled=True)  89 us
    scatter-add x1, other arithmetic, place_terms(): return summed.at[rows, index].add(terms, mode='drop')  52.4 us
    gather x2, local copies, waits for them, and re-layouts, local(): chosen = jnp.take(piece_blocks[:, 0], local_index, axis=0)  33.5 us
    dot_general x1, local copies, waits for them, and re-layouts, local(): jnp.einsum('isxy,isyz->isxz', panel_blocks, chosen, preferred_element_typ...  24.7 us
    dot_general x1, matrix products, local(): jnp.einsum('isxy,isyz->isxz', panel_blocks, chosen, preferred_element_typ...  22.1 us
    squeeze x1, blocking collectives, local(): targets = jnp.take(piece_cols[:, 0], local_index, axis=0) - row_rank * NJR  11.1 us
    all_gather x1, blocking collectives, local(): lax.all_gather(left_cols, 'row', axis=1, tiled=True)  9.8 us
  transfers between devices with their start and end apart: 2, of which 2 were waited for; matrix products, arithmetic and copies ran while one was open for 10% of the time, Pallas kernels for 0%

commit v1 on v0

--- a/solution.py
+++ b/solution.py
@@ -4,6 +4,19 @@
 from jax.sharding import PartitionSpec as P
 
 NJR = 32
+
+
+def collect(x, axis, dim):
+    ways = lax.axis_size(axis)
+    up = [(d, (d + 1) % ways) for d in range(ways)]
+    down = [(d, (d - 1) % ways) for d in range(ways)]
+    earlier, later = ([x], [x])
+    for _ in range(ways // 2):
+        earlier.append(lax.ppermute(earlier[-1], axis, up))
+    for _ in range((ways - 1) // 2):
+        later.append(lax.ppermute(later[-1], axis, down))
+    line = jnp.concatenate([*earlier[::-1], *later[1:]], axis=dim)
+    return jnp.roll(line, (lax.axis_index(axis) - ways // 2) * x.shape[dim], axis=dim)
 
 
 def slot_index(targets, kept):
@@ -33,7 +46,7 @@
         jnp.float32,
     )
     start = jnp.int32(0)
-    piece_blocks = lax.all_gather(right_blocks, "col", axis=0, tiled=True)
+    piece_blocks = collect(right_blocks, "col", 0)
     piece_cols = lax.all_gather(right_cols, "col", axis=0, tiled=True)
     local_index = panel_cols - start
     chosen = jnp.take(piece_blocks[:, 0], local_index, axis=0)

time: 395 us -> 368 us (0.932)
  waiting for transfers between devices: 218 us -> 120 us
  local copies, waits for them, and re-layouts: 63.7 us -> 97.6 us
  blocking collectives: 20.9 us -> 47 us
  starting transfers between devices: 0.04 us -> 10.1 us
    all_gather x1 -> x0, waiting for transfers between devices: 128 us -> none  [local(): piece_blocks = lax.all_gather(right_blocks, 'col', axis=0, tiled=True)]
    ppermute x0 -> x7, waiting for transfers between devices: none -> 119 us  [the longest x4 119 us: collect(): earlier.append(lax.ppermute(earlier[-1], axis, up))]
    all_gather x1, waiting for transfers between devices: 89 us -> 0.01 us  [local(): lax.all_gather(left_blocks, 'row', axis=1, tiled=True)]
    squeeze x1, blocking collectives: 11.1 us -> 38.5 us  [local(): targets = jnp.take(piece_cols[:, 0], local_index, axis=0) - row_rank * NJR]
    unnamed x5 -> x28, local copies, waits for them, and re-layouts: 2.01 us -> 27.4 us
    ppermute x0 -> x7, starting transfers between devices: none -> 10.1 us  [the longest x3 9.57 us: collect(): later.append(lax.ppermute(later[-1], axis, down))]
    squeeze x0 -> x1, local copies, waits for them, and re-layouts: none -> 6.51 us  [local(): chosen = jnp.take(piece_blocks[:, 0], local_index, axis=0)]
  transfers between devices with their start and end apart: 2 -> 8, of which waited for: 2 -> 3; matrix products, arithmetic and copies ran while one was open for 10% -> 19% of each run, Pallas kernels for 0% -> 0%
where the time goes in v1:
time: 368 us; the launch traced here: 366 us
  waiting for transfers between devices  120 us (33%)
  local copies, waits for them, and re-layouts  97.6 us (27%)
  other arithmetic  54.7 us (15%)
  blocking collectives  47 us (13%)
  matrix products  22.1 us (6%)
  between operations  14.3 us (4%)
  starting transfers between devices  10.1 us (3%)
    ppermute x4, waiting for transfers between devices, collect(): earlier.append(lax.ppermute(earlier[-1], axis, up))  119 us
    scatter-add x1, other arithmetic, place_terms(): return summed.at[rows, index].add(terms, mode='drop')  52.4 us
    squeeze x1, blocking collectives, local(): targets = jnp.take(piece_cols[:, 0], local_index, axis=0) - row_rank * NJR  38.5 us
    gather x2, local copies, waits for them, and re-layouts, local(): chosen = jnp.take(piece_blocks[:, 0], local_index, axis=0)  33.6 us
    unnamed x28, local copies, waits for them, and re-layouts  27.4 us
    dot_general x1, local copies, waits for them, and re-layouts, local(): jnp.einsum('isxy,isyz->isxz', panel_blocks, chosen, preferred_element_typ...  24.6 us
    dot_general x1, matrix products, local(): jnp.einsum('isxy,isyz->isxz', panel_blocks, chosen, preferred_element_typ...  22.1 us
    ppermute x3, starting transfers between devices, collect(): later.append(lax.ppermute(later[-1], axis, down))  9.57 us
  transfers between devices with their start and end apart: 8, of which 3 were waited for; matrix products, arithmetic and copies ran while one was open for 19% of the time, Pallas kernels for 0%

profile of v1, /device:TPU:0, one launch (start us, length us, event | category | flops | bytes accessed | tf_op | source)
XLA Modules:
  0.0 365.9 jit_solution(4340983148164523889)
XLA Ops:
  6.5 0.7 all-gather.2.cloned.1.call-update
  7.3 0.5 collective-permute-start
  7.8 28.0 %collective-permute-done = bf16[64,1,128,128]{3,2,1,0:T(8,128)(2,1)S(1)} collective-permute-done((bf16[64,1,128,128]{3,2,1,0:T(8,128)(2,1)}, bf16[64,1,128,128]{3,2,1,0:T(8,128)(2,1)S(1)}, u32[]{:S(2)}, u32[]{:S(2)}) %collective-permute-start) | collective-permute-done | bytes 2097184 | tf_op jit(solution)/shard_map/ppermute | solution.py:15
  35.8 1.3 copy-done.1
  37.1 0.0 collective-permute-start.1
  37.1 3.5 collective-permute-start.4
  40.6 45.3 %collective-permute-done.1 = bf16[64,1,128,128]{3,2,1,0:T(8,128)(2,1)S(1)} collective-permute-done((bf16[64,1,128,128]{3,2,1,0:T(8,128)(2,1)S(1)}, bf16[64,1,128,128]{3,2,1,0:T(8,128)(2,1)S(1)}, u32[]{:S(2)}, u32[]{:S(2)}) %collective-permute-start.1) | collective-permute-done | bytes 2097184 | tf_op jit(solution)/shard_map/ppermute | solution.py:15
  85.9 1.3 copy-done.3
  87.2 3.5 collective-permute-start.5
  90.8 46.1 %collective-permute-done.2 = bf16[64,1,128,128]{3,2,1,0:T(8,128)(2,1)} collective-permute-done((bf16[64,1,128,128]{3,2,1,0:T(8,128)(2,1)S(1)}, bf16[64,1,128,128]{3,2,1,0:T(8,128)(2,1)}, u32[]{:S(2)}, u32[]{:S(2)}) %collective-permute-start.2) | collective-permute-done | bytes 2097184 | tf_op jit(solution)/shard_map/ppermute | solution.py:15
  136.9 8.5 %all_gather.9 = s32[12,32]{0,1:T(8,128)S(1)} all-gather(s32[12,8]{0,1:T(8,128)} %param.6), channel_id=1, replica_groups=mesh['row'=4,'col'=8] {'row'}, dimensions={1}, use_global_device_ids=true | all-gather | bytes 1920 | tf_op jit(solution)/shard_map/all_gather | solution.py:42
  145.4 0.1 copy.20
  145.5 0.1 reshape.46
  145.6 1.2 dynamic-slice
  147.5 0.8 bitcast_dynamic-update-slice_fusion
  148.2 2.5 collective-permute-start.6
  150.7 38.5 %all-reduce = s32[512]{0:T(512)S(1)} all-reduce(s32[512]{0:T(512)S(1)} %bitcast_dynamic-update-slice_fusion), channel_id=1, replica_groups=mesh['row'=4,'col'=8] {'col'}, use_global_device_ids=true, to_apply=%add | all-reduce | flops 512 | bytes 4096 | tf_op jit(solution)/shard_map/squeeze | solution.py:53
  189.2 2.8 gather_fusion
  192.0 0.1 reshape.45
  192.1 0.7 broadcast_subtract_fusion
  192.8 0.1 copy.23
  192.9 0.1 fusion.4
  193.0 0.1 compare_reduce_fusion
  193.1 0.1 reshape.60
  193.2 1.9 constant_dynamic-update-slice_fusion.15
  195.1 2.0 constant_dynamic-update-slice_fusion.14
  197.1 2.0 constant_dynamic-update-slice_fusion.13
  199.1 2.0 constant_dynamic-update-slice_fusion.12
  201.0 0.3 constant_dynamic-update-slice_fusion.11
  201.3 2.0 constant_dynamic-update-slice_fusion.10
  203.3 2.0 constant_dynamic-update-slice_fusion.9
  205.3 2.0 constant_dynamic-update-slice_fusion.8
  207.3 2.0 constant_dynamic-update-slice_fusion.7
  209.3 2.0 constant_dynamic-update-slice_fusion.6
  211.2 0.3 constant_dynamic-update-slice_fusion.5
  211.5 0.3 constant_dynamic-update-slice_fusion.4
  211.8 0.3 constant_dynamic-update-slice_fusion.3
  212.1 2.0 constant_dynamic-update-slice_fusion.2
  214.1 2.0 constant_dynamic-update-slice_fusion.1
  216.1 2.0 constant_dynamic-update-slice_fusion
  218.0 6.5 %dynamic-slice_bitcast_fusion = bf16[512,128,128]{2,1,0:T(8,128)(2,1)} fusion(bf16[1024,1,128,128]{3,2,1,0:T(8,128)(2,1)S(1)} %constant_dynamic-update-slice_fusion, s32[]{:T(128)S(6)} %select_n.62), kind=kLoop, calls=%fused_computation.3 | loop fusion | bytes 33554436 | tf_op jit(solution)/shard_map/squeeze | solution.py:52
  224.5 16.8 %gather_fusion.1 = bf16[384,128,128]{2,1,0:T(8,128)(2,1)} fusion(bf16[512,128,128]{2,1,0:T(8,128)(2,1)} %dynamic-slice_bitcast_fusion, s32[1024]{0:T(1024)S(1)} %pad_clamp_fusion), kind=kCustom, calls=%fused_computation.1 | custom fusion | bytes 25167360 | tf_op jit(solution)/shard_map/jit(_take)/gather | solution.py:52
  241.4 16.7 %copy.24 = bf16[12,32,128,128]{2,3,1,0:T(8,128)(2,1)} copy(bf16[12,32,128,128]{3,2,1,0:T(8,128)(2,1)} %bitcast.17) | data formatting | bytes 25165824 | tf_op jit(solution)/shard_map/jit(_take)/gather | solution.py:52
  258.1 22.1 %fusion = f32[12,32,128,128]{3,2,1,0:T(8,128)} fusion(bf16[12,32,128,128]{3,2,1,0:T(8,128)(2,1)} %all-gather.2.cloned.1.call-done, bf16[12,32,128,128]{2,3,1,0:T(8,128)(2,1)} %copy.24, pred[12,32]{1,0:T(8,128)(4,1)S(1)} %get-tuple-element.6), kind=kOutput, calls=%fused_computation.4 | convolution fusion | flops 1616904192 | bytes 50332032 | tf_op jit(solution)/shard_map/isxy,isyz->isxz/dot_general | solution.py:54
  280.2 24.6 %copy.25 = f32[384,128,128]{2,1,0:T(8,128)} copy(f32[384,128,128]{1,2,0:T(8,128)} %bitcast.16) | data formatting | bytes 50331648 | tf_op jit(solution)/shard_map/isxy,isyz->isxz/dot_general | solution.py:54
  304.9 0.4 broadcast_in_dim.38
  305.2 52.4 %scatter_fusion = f32[12,4,128,128]{3,2,1,0:T(8,128)S(1)} fusion(f32[12,4,128,128]{3,2,1,0:T(8,128)S(1)} %broadcast_in_dim.38, s32[384]{0:T(512)S(1)} %reshape.60, f32[384,128,128]{2,1,0:T(8,128)} %copy.25), kind=kCustom, calls=%fused_computation.2 | custom fusion | flops 6291456 | bytes 75500544 | tf_op jit(solution)/shard_map/scatter-add | solution.py:34
  357.7 1.4 convert_element_type.4
  (21 shorter events, 0.1 us)
Async XLA Ops:
  6.5 194.5 %copy-start = (bf16[64,1,128,128]{3,2,1,0:T(8,128)(2,1)S(1)}, bf16[64,1,128,128]{3,2,1,0:T(8,128)(2,1)}, u32[]{:S(2)}) copy-start(bf16[64,1,128,128]{3,2,1,0:T(8,128)(2,1)} %param.7) | copy-start | bytes 6291460
  6.5 251.6 %all-gather.2.cloned.1.call-start = ((), (), s32[]{:S(2)}) async-start(), calls=%async_computation | async-start | bytes 15728640 | tf_op jit(solution)/shard_map/all_gather | solution.py:41
  7.3 28.5 %collective-permute-start = (bf16[64,1,128,128]{3,2,1,0:T(8,128)(2,1)}, bf16[64,1,128,128]{3,2,1,0:T(8,128)(2,1)S(1)}, u32[]{:S(2)}, u32[]{:S(2)}) collective-permute-start(bf16[64,1,128,128]{3,2,1,0:T(8,128)(2,1)} %param.7), channel_id=1, source_target_pairs={{0,1},{1,2},{2,3},{3,4},{4,5},{5,6},{6,7},{7,0},{8,9},{9,10},{10,1... | collective-permute-start | bytes 6291464 | tf_op jit(solution)/shard_map/ppermute | solution.py:15
  35.8 1.3 copy-start.1
  37.1 48.8 %collective-permute-start.1 = (bf16[64,1,128,128]{3,2,1,0:T(8,128)(2,1)S(1)}, bf16[64,1,128,128]{3,2,1,0:T(8,128)(2,1)S(1)}, u32[]{:S(2)}, u32[]{:S(2)}) collective-permute-start(bf16[64,1,128,128]{3,2,1,0:T(8,128)(2,1)S(1)} %collective-permute-done), channel_id=1, source_target_pairs={{0,1},{1,2},{2,3},{3,4},{4,5},{5,6},{6,7},{7,0},{8,9},{9,10},{10,1... | collective-permute-start | bytes 6291464 | tf_op jit(solution)/shard_map/ppermute | solution.py:15
  37.1 50.1 %collective-permute-start.4 = (bf16[64,1,128,128]{3,2,1,0:T(8,128)(2,1)}, bf16[64,1,128,128]{3,2,1,0:T(8,128)(2,1)}, u32[]{:S(2)}, u32[]{:S(2)}) collective-permute-start(bf16[64,1,128,128]{3,2,1,0:T(8,128)(2,1)} %param.7), channel_id=1, source_target_pairs={{0,7},{1,0},{2,1},{3,2},{4,3},{5,4},{6,5},{7,6},{8,15},{9,8},{10,9... | collective-permute-start | bytes 6291464 | tf_op jit(solution)/shard_map/ppermute | solution.py:17
  85.9 1.3 copy-start.3
  87.2 49.7 %collective-permute-start.2 = (bf16[64,1,128,128]{3,2,1,0:T(8,128)(2,1)S(1)}, bf16[64,1,128,128]{3,2,1,0:T(8,128)(2,1)}, u32[]{:S(2)}, u32[]{:S(2)}) collective-permute-start(bf16[64,1,128,128]{3,2,1,0:T(8,128)(2,1)S(1)} %collective-permute-done.1), channel_id=1, source_target_pairs={{0,1},{1,2},{2,3},{3,4},{4,5},{5,6},{6,7},{7,0},{8,9},{9,10},{10,1... | collective-permute-start | bytes 6291464 | tf_op jit(solution)/shard_map/ppermute | solution.py:15
  87.2 61.0 %collective-permute-start.5 = (bf16[64,1,128,128]{3,2,1,0:T(8,128)(2,1)}, bf16[64,1,128,128]{3,2,1,0:T(8,128)(2,1)}, u32[]{:S(2)}, u32[]{:S(2)}) collective-permute-start(bf16[64,1,128,128]{3,2,1,0:T(8,128)(2,1)} %collective-permute-done.4), channel_id=1, source_target_pairs={{0,7},{1,0},{2,1},{3,2},{4,3},{5,4},{6,5},{7,6},{8,15},{9,8},{10,9... | collective-permute-start | bytes 6291464 | tf_op jit(solution)/shard_map/ppermute | solution.py:17
  136.9 56.3 %collective-permute-start.3 = (bf16[64,1,128,128]{3,2,1,0:T(8,128)(2,1)}, bf16[64,1,128,128]{3,2,1,0:T(8,128)(2,1)}, u32[]{:S(2)}, u32[]{:S(2)}) collective-permute-start(bf16[64,1,128,128]{3,2,1,0:T(8,128)(2,1)} %collective-permute-done.2), channel_id=1, source_target_pairs={{0,1},{1,2},{2,3},{3,4},{4,5},{5,6},{6,7},{7,0},{8,9},{9,10},{10,1... | collective-permute-start | bytes 6291464 | tf_op jit(solution)/shard_map/ppermute | solution.py:15
  148.2 57.0 %collective-permute-start.6 = (bf16[64,1,128,128]{3,2,1,0:T(8,128)(2,1)}, bf16[64,1,128,128]{3,2,1,0:T(8,128)(2,1)}, u32[]{:S(2)}, u32[]{:S(2)}) collective-permute-start(bf16[64,1,128,128]{3,2,1,0:T(8,128)(2,1)} %collective-permute-done.5), channel_id=1, source_target_pairs={{0,7},{1,0},{2,1},{3,2},{4,3},{5,4},{6,5},{7,6},{8,15},{9,8},{10,9... | collective-permute-start | bytes 6291464 | tf_op jit(solution)/shard_map/ppermute | solution.py:17
  193.2 18.0 %copy-start.4 = (bf16[64,1,128,128]{3,2,1,0:T(8,128)(2,1)S(1)}, bf16[64,1,128,128]{3,2,1,0:T(8,128)(2,1)}, u32[]{:S(2)}) copy-start(bf16[64,1,128,128]{3,2,1,0:T(8,128)(2,1)} %copy-done.3) | copy-start | bytes 6291460
  193.2 18.3 %copy-start.2 = (bf16[64,1,128,128]{3,2,1,0:T(8,128)(2,1)S(1)}, bf16[64,1,128,128]{3,2,1,0:T(8,128)(2,1)}, u32[]{:S(2)}) copy-start(bf16[64,1,128,128]{3,2,1,0:T(8,128)(2,1)} %copy-done.1) | copy-start | bytes 6291460
Sparse Core Ops, SparseCore 0:
  9.2 125.1 all-gather.1
